TPU v7x, 512 devices: a whole 4x4x16 slice. The times are simulated.
512 devices in a mesh: sec: 2 (over core), seq: 32 (over z, y_lo), rep: 8 (over x, y_hi).
Axes of the slice: x: 4, y: 4 (y_hi: 2, y_lo: 2; y = y_hi * 2 + y_lo), z: 16, core: 2. Of those that a mesh axis runs over, the one named last changes fastest.
Arguments:
- head_query: bfloat16 [64, 24, 1536, 128], P(('sec', 'rep'), None, 'seq'), may hold values from -4.5 to 4.5
- head_keys: bfloat16 [64, 24, 1536, 128], P(('sec', 'rep'), None, 'seq'), may hold values from -4.5 to 4.5
- head_values: bfloat16 [64, 24, 1536, 128], P(('sec', 'rep'), None, 'seq'), may hold values from -6 to 6
- mod_shift: float32 [64, 3072], P(('sec', 'rep')), may hold values from -3 to 3
- mod_scale: float32 [64, 3072], P(('sec', 'rep')), may hold values from -0.9 to 0.9
- final_weight: bfloat16 [3072, 64], replicated, may hold values from -0.109375 to 0.109375
- final_bias: float32 [64], replicated, may hold values from -3 to 3
- noisy_latent: float32 [64, 3, 64, 512], P(('sec', 'rep'), None, 'seq'), may hold values from -7.2 to 7.2
- step_index: int32 [64], P(('sec', 'rep')), may hold values from 46 to 49
- clip_order: int32 [64], replicated, may hold values from 0 to 63, each once
- conv_weight: bfloat16 [3, 3, 3, 16, 512], replicated, may hold values from -0.3125 to 0.3125
- conv_bias: float32 [512], replicated, may hold values from -3 to 3
- group_gain: float32 [512], replicated, may hold values from 0.1 to 1.9
- group_shift: float32 [512], replicated, may hold values from -3 to 3
Outputs:
- denoised: float32 [64, 3, 64, 512], P(('sec', 'rep'), None, 'seq')
- features: bfloat16 [64, 3, 64, 16384], P(('sec', 'rep'), None, 'seq')
All inputs are finite; a program needn't handle non-finite values.
Results may differ from a plain program's by a relative error of at most 0.005.
Values may be sent and summed in bfloat16 or wider, within the bound.
No kernel may reach another device: no remote copies, remote signals or barrier semaphores. Data moves between devices by JAX's collectives and lax.ppermute only.
A program may use at most 128 MiB of HBM per device.

v0:
```python
import math
import jax
import jax.numpy as jnp
from jax import lax
from jax.sharding import PartitionSpec as P

HEADS = 24
HEAD_DIM = 128
LAT_CH = 16
VAE_CH = 512
GROUPS = 32
FRAMES = 3
PATCH_W = 16
NSTEPS = 50
PATCH_OUT = 64
LAT_W = 32
eps_norm = 1e-06
shift_factor = 7.0


def extended(cells, sides, width):
    for axis, dim in sides:
        count = lax.axis_size(axis)
        ends = count - 1
        head = lax.slice_in_dim(cells, 0, width, axis=dim)
        tail = lax.slice_in_dim(cells, cells.shape[dim] - width, cells.shape[dim], axis=dim)
        cells = jnp.concatenate(
            [
                lax.ppermute(tail, axis, [(i, (i + 1) % count) for i in range(ends)]),
                cells,
                lax.ppermute(head, axis, [((i + 1) % count, i) for i in range(ends)]),
            ],
            axis=dim,
        )
    return cells


def attend_unit(operands):
    query_rows, key_rows, value_rows = operands
    length = query_rows.shape[0]
    block = math.gcd(length, 512)
    scale = 1.0 / math.sqrt(query_rows.shape[1])
    blocks = query_rows.reshape(length // block, block, query_rows.shape[1])

    def one_block(rows):
        scores = jnp.dot(rows, key_rows.T, preferred_element_type=jnp.float32) * scale
        top = jnp.max(scores, axis=1, keepdims=True)
        expd = jnp.exp(scores - top)
        weights = (expd / jnp.sum(expd, axis=1, keepdims=True)).astype(jnp.bfloat16)
        return jnp.dot(weights, value_rows, preferred_element_type=jnp.float32).astype(jnp.bfloat16)

    return lax.map(one_block, blocks).reshape(length, query_rows.shape[1])


def sigma_level(index):
    level = 1.0 - index.astype(jnp.float32) / NSTEPS
    return shift_factor * level / (1.0 + (shift_factor - 1.0) * level)


def causal_columns(rimmed):
    clips, frames, rows_rim, wide = rimmed.shape
    width = wide // LAT_CH
    grid = rimmed.reshape(clips, frames, rows_rim, width, LAT_CH)
    first = grid[:, :1]
    grid = jnp.concatenate([first, first, grid], axis=1)
    grid = jnp.pad(grid, ((0, 0), (0, 0), (0, 0), (1, 1), (0, 0)), mode="edge")
    taps = []
    for tap_time in range(3):
        for tap_row in range(3):
            for tap_col in range(3):
                taps.append(
                    grid[
                        :,
                        tap_time : tap_time + frames,
                        tap_row : tap_row + rows_rim - 2,
                        tap_col : tap_col + width,
                        :,
                    ]
                )
    return jnp.stack(taps, axis=4).reshape(clips, frames, rows_rim - 2, width, 27 * LAT_CH)


def edge_rows(rimmed):
    position = lax.axis_index("seq")
    last_index = lax.axis_size("seq") - 1
    upper = jnp.where(position == 0, rimmed[:, :, 1:2], rimmed[:, :, 0:1])
    lower = jnp.where(position == last_index, rimmed[:, :, -2:-1], rimmed[:, :, -1:])
    return jnp.concatenate([upper, rimmed[:, :, 1:-1], lower], axis=2)


def shards(
    head_query,
    head_keys,
    head_values,
    mod_shift,
    mod_scale,
    final_weight,
    final_bias,
    noisy_latent,
    step_index,
    clip_order,
    conv_weight,
    conv_bias,
    group_gain,
    group_shift,
):
    n_seq = lax.axis_size("seq")
    clips = head_query.shape[0]
    tok_dev = head_query.shape[2]
    units_local = clips * HEADS // n_seq
    query_four = head_query.reshape(n_seq, units_local, tok_dev, HEAD_DIM)
    keys_four = head_keys.reshape(n_seq, units_local, tok_dev, HEAD_DIM)
    values_four = head_values.reshape(n_seq, units_local, tok_dev, HEAD_DIM)
    query_part = lax.all_to_all(query_four, "seq", split_axis=0, concat_axis=2, tiled=True)
    keys_part = lax.all_to_all(keys_four, "seq", split_axis=0, concat_axis=2, tiled=True)
    values_part = lax.all_to_all(values_four, "seq", split_axis=0, concat_axis=2, tiled=True)
    outputs = lax.map(attend_unit, (query_part[0], keys_part[0], values_part[0]))[None]
    mixed = lax.all_to_all(outputs, "seq", split_axis=2, concat_axis=0, tiled=True)
    weights3 = final_weight.astype(jnp.float32).reshape(HEADS, HEAD_DIM, PATCH_OUT)
    scale3 = mod_scale.reshape(clips, HEADS, HEAD_DIM)
    shift3 = mod_shift.reshape(clips, HEADS, HEAD_DIM)
    heads = mixed.reshape(clips, HEADS, tok_dev, HEAD_DIM).astype(jnp.float32)
    mean = jnp.mean(heads, axis=(1, 3), keepdims=True)
    spread = jnp.mean(jnp.square(heads - mean), axis=(1, 3), keepdims=True)
    normed = (heads - mean) * lax.rsqrt(spread + eps_norm)
    modulated = normed * (1.0 + scale3[:, :, None, :]) + shift3[:, :, None, :]
    velocity = (
        jnp.einsum("chtd,hdo->cto", modulated, weights3, precision=lax.Precision.HIGHEST)
        + final_bias
    )
    rows_dev = noisy_latent.shape[2]
    velocity = velocity.reshape(clips, rows_dev // 2, FRAMES, PATCH_W, 2, 2, LAT_CH)
    velocity = jnp.transpose(velocity, (0, 2, 1, 4, 3, 5, 6)).reshape(noisy_latent.shape)
    step = sigma_level(step_index + 1) - sigma_level(step_index)
    denoised = noisy_latent + step[:, None, None, None] * velocity
    decoder_in = denoised.astype(jnp.bfloat16)
    group_index = lax.axis_index(("sec", "rep"))
    wanted = lax.dynamic_slice_in_dim(clip_order, group_index * clips, clips)
    everyone = lax.all_gather(decoder_in, ("sec", "rep"), axis=0, tiled=True)
    picked = jnp.take(everyone, wanted, axis=0)
    rimmed = edge_rows(extended(picked, (("seq", 2),), 1))
    columns = causal_columns(rimmed)
    flat_weight = conv_weight.reshape(27 * LAT_CH, VAE_CH)
    conv_out = (
        jnp.dot(columns.reshape(-1, 27 * LAT_CH), flat_weight, preferred_element_type=jnp.float32)
        + conv_bias
    )
    conv_out = conv_out.reshape(clips, -1, GROUPS, VAE_CH // GROUPS)
    cells = conv_out.shape[1] * n_seq * (VAE_CH // GROUPS)
    local_sum = jnp.sum(conv_out, axis=(1, 3))
    mean = lax.psum(local_sum, "seq") / cells
    centered = conv_out - mean[:, None, :, None]
    spread = lax.psum(jnp.sum(jnp.square(centered), axis=(1, 3)), "seq") / cells
    normed = (centered * lax.rsqrt(spread + eps_norm)[:, None, :, None]).reshape(clips, -1, VAE_CH)
    features = jax.nn.silu(normed * group_gain + group_shift).astype(jnp.bfloat16)
    features = features.reshape(clips, FRAMES, rows_dev, LAT_W * VAE_CH)
    return (denoised, features)


def solution(mesh):
    placed = (
        P(("sec", "rep"), None, "seq", None),
        P(("sec", "rep"), None, "seq", None),
        P(("sec", "rep"), None, "seq", None),
        P(("sec", "rep"), None),
        P(("sec", "rep"), None),
        P(),
        P(),
        P(("sec", "rep"), None, "seq", None),
        P(("sec", "rep")),
        P(),
        P(),
        P(),
        P(),
        P(),
    )
    return jax.shard_map(
        shards,
        mesh=mesh,
        in_specs=placed,
        out_specs=(P(("sec", "rep"), None, "seq", None), P(("sec", "rep"), None, "seq", None)),
        check_vma=False,
    )
```

profile of v0, /device:TPU:8, one launch (start us, length us, event | category | flops | bytes accessed | tf_op | source)
XLA Modules:
  0.0 569.3 jit_solution(6883211467850710125)
XLA Ops:
  0.7 77.9 %all_to_all.54 = bf16[32,3,48,128]{3,2,1,0:T(8,128)(2,1)} all-to-all(bf16[32,3,48,128]{3,2,1,0:T(8,128)(2,1)} %bitcast.227), channel_id=1, replica_groups=mesh['sec'=2,'seq'=32,'rep'=8] {'seq'}, dimensions={0} | all-to-all | bytes 2359296 | tf_op jit(solution)/shard_map/all_to_all | solution.py:114
  78.5 64.2 %all_to_all.55 = bf16[32,3,48,128]{3,2,1,0:T(8,128)(2,1)} all-to-all(bf16[32,3,48,128]{3,2,1,0:T(8,128)(2,1)S(1)} %bitcast.228), channel_id=1, replica_groups=mesh['sec'=2,'seq'=32,'rep'=8] {'seq'}, dimensions={0} | all-to-all | bytes 2359296 | tf_op jit(solution)/shard_map/all_to_all | solution.py:115
  142.7 4.2 all-to-all-start.2
  146.9 1.4 copy.116
  149.6 55.0 %all-to-all-done.2 = bf16[32,3,48,128]{3,2,1,0:T(8,128)(2,1)S(1)} async-done(((bf16[32,3,48,128]{3,2,1,0:T(8,128)(2,1)}), bf16[32,3,48,128]{3,2,1,0:T(8,128)(2,1)S(1)}, u32[]{:S(2)}, u32[]{:S(2)}) %all-to-all-start.2) | async-done | bytes 1179680 | tf_op jit(solution)/shard_map/all_to_all | solution.py:116
  205.8 24.2 %while.21 = (s32[]{:T(128)}, bf16[3,1536,128]{2,1,0:T(8,128)(2,1)}, bf16[3,1536,128]{2,1,0:T(8,128)(2,1)S(1)}, bf16[3,1536,128]{2,1,0:T(8,128)(2,1)}, bf16[3,153...) while((s32[]{:T(128)}, bf16[3,1536,128]{2,1,0:T(8,128)(2,1)}, ...), condition=%wide.region_5.6_spmd, body=%wide.region_0.5_spmd.sunk | while | flops 408222720 | bytes 13641974 | solution.py:117
  205.8 1.2 dynamic-slice_bitcast_fusion.3
  207.0 6.1 %while.22 = (s32[]{:T(128)}, bf16[3,512,128]{2,1,0:T(8,128)(2,1)S(1)}, bf16[3,512,128]{2,1,0:T(8,128)(2,1)S(1)}, bf16[1536,128]{1,0:T(8,128)(2,1)S(1)}, bf16[1536,128]{1,0:T(8,128)(2,1)S(1)}, /*index=5*/s32[]{:T(128)}) while((s32[]{:T(128)}, bf16[3,512,128]{2,1,0:T(8,128)(2,1)S(1)}, bf16[3,512,128]{2,1,0:T(8,128)(2,1)S(1)}, ...), condition=%wide.region_4.4_spmd, body=%wide.region_1.3_spmd.sunk | while | flops 408222720 | bytes 10496085 | solution.py:52
  213.8 1.2 dynamic-slice_bitcast_fusion.3
  215.0 6.1 %while.22 = (s32[]{:T(128)}, bf16[3,512,128]{2,1,0:T(8,128)(2,1)S(1)}, bf16[3,512,128]{2,1,0:T(8,128)(2,1)S(1)}, bf16[1536,128]{1,0:T(8,128)(2,1)S(1)}, bf16[1536,128]{1,0:T(8,128)(2,1)S(1)}, /*index=5*/s32[]{:T(128)}) while((s32[]{:T(128)}, bf16[3,512,128]{2,1,0:T(8,128)(2,1)S(1)}, bf16[3,512,128]{2,1,0:T(8,128)(2,1)S(1)}, ...), condition=%wide.region_4.4_spmd, body=%wide.region_1.3_spmd.sunk | while | flops 408222720 | bytes 10496085 | solution.py:52
  223.1 6.1 %while.22 = (s32[]{:T(128)}, bf16[3,512,128]{2,1,0:T(8,128)(2,1)S(1)}, bf16[3,512,128]{2,1,0:T(8,128)(2,1)S(1)}, bf16[1536,128]{1,0:T(8,128)(2,1)S(1)}, bf16[1536,128]{1,0:T(8,128)(2,1)S(1)}, /*index=5*/s32[]{:T(128)}) while((s32[]{:T(128)}, bf16[3,512,128]{2,1,0:T(8,128)(2,1)S(1)}, bf16[3,512,128]{2,1,0:T(8,128)(2,1)S(1)}, ...), condition=%wide.region_4.4_spmd, body=%wide.region_1.3_spmd.sunk | while | flops 408222720 | bytes 10496085 | solution.py:52
  229.9 8.1 %copy.141 = bf16[3,1536,128]{2,0,1:T(4,128)(2,1)} copy(bf16[3,1536,128]{2,1,0:T(8,128)(2,1)} %get-tuple-element.56) | data formatting | bytes 2359296 | tf_op jit(solution)/shard_map/while | solution.py:117
  238.1 5.7 all-to-all-start.3
  243.9 76.1 %all-to-all-done.3 = bf16[1,3,1536,128]{3,1,0,2:T(4,128)(2,1)S(1)} async-done(((bf16[1,3,1536,128]{3,1,0,2:T(4,128)(2,1)}), bf16[1,3,1536,128]{3,1,0,2:T(4,128)(2,1)S(1)}, u32[]{:S(2)}, u32[]{:S(2)}) %all-to-all-start.3) | async-done | bytes 1179680 | tf_op jit(solution)/shard_map/all_to_all | solution.py:118
  320.4 3.1 fusion.19
  323.7 22.0 %multiply_reduce_fusion = f32[32,48]{1,0:T(8,128)S(1)} fusion(bf16[1,3,32,48,128]{4,1,3,2,0:T(4,128)(2,1)S(1)} %bitcast.219, f32[32,48]{1,0:T(8,128)S(1)} %broadcast_bitcast_fusion.2), kind=kLoop, calls=%fused_computation.17 | loop fusion | flops 2357760 | bytes 1191936 | tf_op jit(solution)/shard_map/reduce_sum | solution.py:124
  345.8 1.6 fusion.28
  349.2 36.8 %all_gather.3 = bf16[64,3,2,512]{3,2,1,0:T(2,128)(2,1)S(1)} all-gather(bf16[4,3,2,512]{3,2,1,0:T(2,128)(2,1)S(1)} %get-tuple-element.79), channel_id=1, replica_groups=mesh['sec'=2,'seq'=32,'rep'=8] {'sec','rep'}, dimensions={0}, use_global_device_ids=true | all-gather | bytes 417792 | tf_op jit(solution)/shard_map/all_gather | solution.py:139
  386.7 3.1 collective-permute-start
  389.8 3.0 collective-permute-start.1
  392.8 3.5 collective-permute-done.1
  416.5 7.9 %copy.123 = bf16[4,3,2,32,27,16]{3,2,1,0,5,4:T(2,128)(2,1)S(1)} copy(bf16[4,3,2,32,27,16]{5,3,2,1,0,4:T(8,128)(2,1)} %fusion.49) | data formatting | bytes 1327104 | tf_op jit(solution)/shard_map/stack | solution.py:80
  424.5 2.5 reshape_reshape.3
  427.0 1.7 convolution_add_fusion
  428.7 1.6 copy.124
  430.3 2.5 reshape.109
  432.8 2.7 reshape.110
  436.0 59.9 %psum.14 = f32[4,32]{1,0:T(4,128)S(1)} all-reduce(f32[4,32]{1,0:T(4,128)S(1)} %copy.125), channel_id=1, replica_groups=mesh['sec'=2,'seq'=32,'rep'=8] {'seq'}, use_global_device_ids=true, to_apply=%region_11.12 | all-reduce | flops 128 | bytes 1024 | tf_op jit(solution)/shard_map/psum | solution.py:151
  496.8 62.3 %psum.15 = f32[4,32]{1,0:T(4,128)S(1)} all-reduce(f32[4,32]{1,0:T(4,128)S(1)} %copy.127), channel_id=1, replica_groups=mesh['sec'=2,'seq'=32,'rep'=8] {'seq'}, use_global_device_ids=true, to_apply=%region_13.14 | all-reduce | flops 128 | bytes 1024 | tf_op jit(solution)/shard_map/psum | solution.py:153
  559.5 2.5 mul.94
  562.3 2.5 sub.70
  564.8 4.5 fusion.20
  (136 shorter events, 49.6 us)
Async XLA Ops:
  0.6 426.3 %copy-start = (bf16[3,3,3,16,512]{4,3,2,1,0:T(8,128)(2,1)S(1)}, bf16[3,3,3,16,512]{4,3,2,1,0:T(8,128)(2,1)}, u32[]{:S(2)}) copy-start(bf16[3,3,3,16,512]{4,3,2,1,0:T(8,128)(2,1)} %param.28) | copy-start | bytes 1327108
  0.6 77.9 %copy-start.2 = (bf16[4,24,48,128]{3,2,1,0:T(8,128)(2,1)S(1)}, bf16[4,24,48,128]{3,2,1,0:T(8,128)(2,1)}, u32[]{:S(2)}) copy-start(bf16[4,24,48,128]{3,2,1,0:T(8,128)(2,1)} %param.19) | copy-start | bytes 3538948
  142.7 61.9 %all-to-all-start.2 = ((bf16[32,3,48,128]{3,2,1,0:T(8,128)(2,1)}), bf16[32,3,48,128]{3,2,1,0:T(8,128)(2,1)S(1)}, u32[]{:S(2)}, u32[]{:S(2)}) async-start(bf16[32,3,48,128]{3,2,1,0:T(8,128)(2,1)} %bitcast.14), calls=%async_computation.2 | async-start | bytes 2359296 | tf_op jit(solution)/shard_map/all_to_all | solution.py:116
  146.9 1.6 copy-start.1
  229.9 13.8 %copy-start.8 = (s32[64]{0:T(128)S(1)}, s32[64]{0:T(128)}, u32[]{:S(2)}) copy-start(s32[64]{0:T(128)} %param.27) | copy-start | bytes 772
  229.9 13.9 %copy-start.11 = (s32[4]{0:T(128)S(1)}, s32[4]{0:T(128)}, u32[]{:S(2)}) copy-start(s32[4]{0:T(128)} %param.26) | copy-start | bytes 52
  229.9 13.9 %copy-start.6 = (f32[512]{0:T(512)S(1)}, f32[512]{0:T(512)}, u32[]{:S(2)}) copy-start(f32[512]{0:T(512)} %param.31) | copy-start | bytes 6148
  229.9 14.0 %copy-start.3 = (f32[4,3072]{1,0:T(4,128)S(1)}, f32[4,3072]{1,0:T(4,128)}, u32[]{:S(2)}) copy-start(f32[4,3072]{1,0:T(4,128)} %param.22) | copy-start | bytes 147460
  229.9 14.0 %copy-start.4 = (f32[4,3072]{1,0:T(4,128)S(1)}, f32[4,3072]{1,0:T(4,128)}, u32[]{:S(2)}) copy-start(f32[4,3072]{1,0:T(4,128)} %param.21) | copy-start | bytes 147460
  238.1 82.0 %all-to-all-start.3 = ((bf16[1,3,1536,128]{3,1,0,2:T(4,128)(2,1)}), bf16[1,3,1536,128]{3,1,0,2:T(4,128)(2,1)S(1)}, u32[]{:S(2)}, u32[]{:S(2)}) async-start(bf16[1,3,1536,128]{3,1,0,2:T(4,128)(2,1)} %bitcast.224), calls=%async_computation.3 | async-start | bytes 3145728 | tf_op jit(solution)/shard_map/all_to_all | solution.py:118
  323.5 22.3 %copy-start.9 = (bf16[3072,64]{0,1:T(8,128)(2,1)S(1)}, bf16[3072,64]{0,1:T(8,128)(2,1)}, u32[]{:S(2)}) copy-start(bf16[3072,64]{0,1:T(8,128)(2,1)} %param.23) | copy-start | bytes 1179652
  323.5 22.3 %copy-start.12 = (f32[64]{0:T(128)S(1)}, f32[64]{0:T(128)}, u32[]{:S(2)}) copy-start(f32[64]{0:T(128)} %param.24) | copy-start | bytes 772
  323.7 24.7 %copy-start.5 = (f32[4,3,2,512]{3,2,1,0:T(2,128)S(1)}, f32[4,3,2,512]{3,2,1,0:T(2,128)}, u32[]{:S(2)}) copy-start(f32[4,3,2,512]{3,2,1,0:T(2,128)} %param.25) | copy-start | bytes 147460
  345.8 47.0 %copy-start.7 = (f32[512]{0:T(512)S(1)}, f32[512]{0:T(512)}, u32[]{:S(2)}) copy-start(f32[512]{0:T(512)} %param.30) | copy-start | bytes 6148
  386.7 6.2 %collective-permute-start = (bf16[4,3,1,512]{3,2,1,0:T(2,128)(2,1)S(1)}, bf16[4,3,1,512]{3,2,1,0:T(2,128)(2,1)S(1)}, u32[]{:S(2)}, u32[]{:S(2)}) collective-permute-start(bf16[4,3,1,512]{3,2,1,0:T(2,128)(2,1)S(1)} %get-tuple-element.89), channel_id=1, source_target_pairs={{0,8},{8,16},{16,24},{24,32},{32,40},{40,48},{48,56},{56,64},{64,7... | collective-permute-start | bytes 36872 | tf_op jit(solution)/shard_map/ppermute | solution.py:29
  389.8 6.6 %collective-permute-start.1 = (bf16[4,3,1,512]{3,2,1,0:T(2,128)(2,1)S(1)}, bf16[4,3,1,512]{3,2,1,0:T(2,128)(2,1)S(1)}, u32[]{:S(2)}, u32[]{:S(2)}) collective-permute-start(bf16[4,3,1,512]{3,2,1,0:T(2,128)(2,1)S(1)} %get-tuple-element.90), channel_id=1, source_target_pairs={{8,0},{16,8},{24,16},{32,24},{40,32},{48,40},{56,48},{64,56},{72,6... | collective-permute-start | bytes 36872 | tf_op jit(solution)/shard_map/ppermute | solution.py:31
  424.4 2.5 copy-start.10
where the time goes:
time: 570 us; the launch traced here: 569 us
  blocking collectives  301 us (53%)
  waiting for transfers between devices  135 us (24%)
  local copies, waits for them, and re-layouts  58.9 us (10%)
  other arithmetic  41.5 us (7%)
  matrix products  16.1 us (3%)
  starting transfers between devices  15.9 us (3%)
    all_to_all x1, blocking collectives, shards(): lax.all_to_all(query_four, 'seq', split_axis=0, concat_axis=2, tiled=True)  77.9 us
    all_to_all x1, waiting for transfers between devices, shards(): lax.all_to_all(outputs, 'seq', split_axis=2, concat_axis=0, tiled=True)  76.1 us
    all_to_all x1, blocking collectives, shards(): lax.all_to_all(keys_four, 'seq', split_axis=0, concat_axis=2, tiled=True)  64.2 us
    psum x1, blocking collectives, shards(): spread = lax.psum(jnp.sum(jnp.square(centered), axis=(1, 3)), 'seq') / cells  62.3 us
    psum x1, blocking collectives, shards(): mean = lax.psum(local_sum, 'seq') / cells  59.9 us
    all_to_all x1, waiting for transfers between devices, shards(): lax.all_to_all(values_four, 'seq', split_axis=0, concat_axis=2, tiled=True)  55 us
    all_gather x1, blocking collectives, shards(): everyone = lax.all_gather(decoder_in, ('sec', 'rep'), axis=0, tiled=True)  36.8 us
    reduce_sum x2, other arithmetic, shards(): spread = jnp.mean(jnp.square(heads - mean), axis=(1, 3), keepdims=True)  22 us
  transfers between devices with their start and end apart: 4, of which 3 were waited for; matrix products, arithmetic and copies ran while one was open for 0% of the time, Pallas kernels for 0%

commit v1 on v0

--- a/solution.py
+++ b/solution.py
@@ -136,7 +136,12 @@
     decoder_in = denoised.astype(jnp.bfloat16)
     group_index = lax.axis_index(("sec", "rep"))
     wanted = lax.dynamic_slice_in_dim(clip_order, group_index * clips, clips)
-    everyone = lax.all_gather(decoder_in, ("sec", "rep"), axis=0, tiled=True)
+    everyone = jnp.concatenate(
+        lax.all_to_all(
+            jnp.stack([decoder_in] * lax.axis_size(("sec", "rep"))), ("sec", "rep"), 0, 0
+        ),
+        axis=0,
+    )
     picked = jnp.take(everyone, wanted, axis=0)
     rimmed = edge_rows(extended(picked, (("seq", 2),), 1))
     columns = causal_columns(rimmed)

time: 570 us -> 552 us (0.968)
  blocking collectives: 301 us -> 264 us
  waiting for transfers between devices: 135 us -> 146 us
  starting transfers between devices: 15.9 us -> 22.3 us
    all_gather x1 -> x0, blocking collectives: 36.8 us -> none  [shards(): everyone = lax.all_gather(decoder_in, ('sec', 'rep'), axis=0, tiled=True)]
    all_to_all x0 -> x1, waiting for transfers between devices: none -> 10.8 us  [shards(): lax.all_to_all(jnp.stack([decoder_in] * lax.axis_size(('sec', 'rep'))), (...]
    all_to_all x0 -> x1, starting transfers between devices: none -> 6.14 us  [shards(): lax.all_to_all(jnp.stack([decoder_in] * lax.axis_size(('sec', 'rep'))), (...]
  transfers between devices with their start and end apart: 4 -> 5, of which waited for: 3 -> 4; matrix products, arithmetic and copies ran while one was open for 0% -> 0% of each run, Pallas kernels for 0% -> 0%
where the time goes in v1:
time: 552 us; the launch traced here: 551 us
  blocking collectives  264 us (48%)
  waiting for transfers between devices  146 us (26%)
  local copies, waits for them, and re-layouts  59.9 us (11%)
  other arithmetic  41.5 us (8%)
  starting transfers between devices  22.3 us (4%)
  matrix products  16.1 us (3%)
    all_to_all x1, blocking collectives, shards(): lax.all_to_all(query_four, 'seq', split_axis=0, concat_axis=2, tiled=True)  77.9 us
    all_to_all x1, waiting for transfers between devices, shards(): lax.all_to_all(outputs, 'seq', split_axis=2, concat_axis=0, tiled=True)  76.2 us
    all_to_all x1, blocking collectives, shards(): lax.all_to_all(keys_four, 'seq', split_axis=0, concat_axis=2, tiled=True)  64.2 us
    psum x1, blocking collectives, shards(): spread = lax.psum(jnp.sum(jnp.square(centered), axis=(1, 3)), 'seq') / cells  62.4 us
    psum x1, blocking collectives, shards(): mean = lax.psum(local_sum, 'seq') / cells  59.7 us
    all_to_all x1, waiting for transfers between devices, shards(): lax.all_to_all(values_four, 'seq', split_axis=0, concat_axis=2, tiled=True)  55 us
    reduce_sum x2, other arithmetic, shards(): spread = jnp.mean(jnp.square(heads - mean), axis=(1, 3), keepdims=True)  22 us
    unnamed x51, local copies, waits for them, and re-layouts  15.2 us
  transfers between devices with their start and end apart: 5, of which 4 were waited for; matrix products, arithmetic and copies ran while one was open for 0% of the time, Pallas kernels for 0%

profile of v1, /device:TPU:8, one launch (start us, length us, event | category | flops | bytes accessed | tf_op | source)
XLA Modules:
  0.0 551.1 jit_solution(3642542454033238650)
XLA Ops:
  0.7 77.9 %all_to_all.59 = bf16[32,3,48,128]{3,2,1,0:T(8,128)(2,1)} all-to-all(bf16[32,3,48,128]{3,2,1,0:T(8,128)(2,1)} %bitcast.228), channel_id=1, replica_groups=mesh['sec'=2,'seq'=32,'rep'=8] {'seq'}, dimensions={0} | all-to-all | bytes 2359296 | tf_op jit(solution)/shard_map/all_to_all | solution.py:114
  78.5 64.2 %all_to_all.60 = bf16[32,3,48,128]{3,2,1,0:T(8,128)(2,1)} all-to-all(bf16[32,3,48,128]{3,2,1,0:T(8,128)(2,1)S(1)} %bitcast.229), channel_id=1, replica_groups=mesh['sec'=2,'seq'=32,'rep'=8] {'seq'}, dimensions={0} | all-to-all | bytes 2359296 | tf_op jit(solution)/shard_map/all_to_all | solution.py:115
  142.7 4.2 all-to-all-start.2
  146.9 1.4 copy.116
  149.6 55.0 %all-to-all-done.2 = bf16[32,3,48,128]{3,2,1,0:T(8,128)(2,1)S(1)} async-done(((bf16[32,3,48,128]{3,2,1,0:T(8,128)(2,1)}), bf16[32,3,48,128]{3,2,1,0:T(8,128)(2,1)S(1)}, u32[]{:S(2)}, u32[]{:S(2)}) %all-to-all-start.2) | async-done | bytes 1179680 | tf_op jit(solution)/shard_map/all_to_all | solution.py:116
  205.8 24.2 %while.21 = (s32[]{:T(128)}, bf16[3,1536,128]{2,1,0:T(8,128)(2,1)}, bf16[3,1536,128]{2,1,0:T(8,128)(2,1)S(1)}, bf16[3,1536,128]{2,1,0:T(8,128)(2,1)}, bf16[3,153...) while((s32[]{:T(128)}, bf16[3,1536,128]{2,1,0:T(8,128)(2,1)}, ...), condition=%wide.region_5.6_spmd, body=%wide.region_0.5_spmd.sunk | while | flops 408222720 | bytes 13641974 | solution.py:117
  205.8 1.2 dynamic-slice_bitcast_fusion.3
  207.0 6.1 %while.22 = (s32[]{:T(128)}, bf16[3,512,128]{2,1,0:T(8,128)(2,1)S(1)}, bf16[3,512,128]{2,1,0:T(8,128)(2,1)S(1)}, bf16[1536,128]{1,0:T(8,128)(2,1)S(1)}, bf16[1536,128]{1,0:T(8,128)(2,1)S(1)}, /*index=5*/s32[]{:T(128)}) while((s32[]{:T(128)}, bf16[3,512,128]{2,1,0:T(8,128)(2,1)S(1)}, bf16[3,512,128]{2,1,0:T(8,128)(2,1)S(1)}, ...), condition=%wide.region_4.4_spmd, body=%wide.region_1.3_spmd.sunk | while | flops 408222720 | bytes 10496085 | solution.py:52
  215.0 6.1 %while.22 = (s32[]{:T(128)}, bf16[3,512,128]{2,1,0:T(8,128)(2,1)S(1)}, bf16[3,512,128]{2,1,0:T(8,128)(2,1)S(1)}, bf16[1536,128]{1,0:T(8,128)(2,1)S(1)}, bf16[1536,128]{1,0:T(8,128)(2,1)S(1)}, /*index=5*/s32[]{:T(128)}) while((s32[]{:T(128)}, bf16[3,512,128]{2,1,0:T(8,128)(2,1)S(1)}, bf16[3,512,128]{2,1,0:T(8,128)(2,1)S(1)}, ...), condition=%wide.region_4.4_spmd, body=%wide.region_1.3_spmd.sunk | while | flops 408222720 | bytes 10496085 | solution.py:52
  223.1 6.1 %while.22 = (s32[]{:T(128)}, bf16[3,512,128]{2,1,0:T(8,128)(2,1)S(1)}, bf16[3,512,128]{2,1,0:T(8,128)(2,1)S(1)}, bf16[1536,128]{1,0:T(8,128)(2,1)S(1)}, bf16[1536,128]{1,0:T(8,128)(2,1)S(1)}, /*index=5*/s32[]{:T(128)}) while((s32[]{:T(128)}, bf16[3,512,128]{2,1,0:T(8,128)(2,1)S(1)}, bf16[3,512,128]{2,1,0:T(8,128)(2,1)S(1)}, ...), condition=%wide.region_4.4_spmd, body=%wide.region_1.3_spmd.sunk | while | flops 408222720 | bytes 10496085 | solution.py:52
  229.9 8.1 %copy.141 = bf16[3,1536,128]{2,0,1:T(4,128)(2,1)} copy(bf16[3,1536,128]{2,1,0:T(8,128)(2,1)} %get-tuple-element.56) | data formatting | bytes 2359296 | tf_op jit(solution)/shard_map/while | solution.py:117
  238.0 6.0 %all-to-all-start.3 = ((bf16[1,3,1536,128]{3,1,0,2:T(4,128)(2,1)}), bf16[1,3,1536,128]{3,1,0,2:T(4,128)(2,1)S(1)}, u32[]{:S(2)}, u32[]{:S(2)}) async-start(bf16[1,3,1536,128]{3,1,0,2:T(4,128)(2,1)} %bitcast.225), calls=%async_computation.3 | async-start | bytes 3145728 | tf_op jit(solution)/shard_map/all_to_all | solution.py:118
  244.1 76.2 %all-to-all-done.3 = bf16[1,3,1536,128]{3,1,0,2:T(4,128)(2,1)S(1)} async-done(((bf16[1,3,1536,128]{3,1,0,2:T(4,128)(2,1)}), bf16[1,3,1536,128]{3,1,0,2:T(4,128)(2,1)S(1)}, u32[]{:S(2)}, u32[]{:S(2)}) %all-to-all-start.3) | async-done | bytes 1179680 | tf_op jit(solution)/shard_map/all_to_all | solution.py:118
  320.6 3.1 fusion.19
  324.0 22.0 %multiply_reduce_fusion = f32[32,48]{1,0:T(8,128)S(1)} fusion(bf16[1,3,32,48,128]{4,1,3,2,0:T(4,128)(2,1)S(1)} %bitcast.220, f32[32,48]{1,0:T(8,128)S(1)} %broadcast_bitcast_fusion.2), kind=kLoop, calls=%fused_computation.17 | loop fusion | flops 2357760 | bytes 1191936 | tf_op jit(solution)/shard_map/reduce_sum | solution.py:124
  346.1 1.6 fusion.28
  350.4 6.1 %all-to-all-start.4 = ((bf16[16,4,3,2,512]{4,3,2,1,0:T(2,128)(2,1)}), bf16[16,4,3,2,512]{4,3,2,1,0:T(2,128)(2,1)S(1)}, u32[]{:S(2)}, u32[]{:S(2)}) async-start(bf16[16,4,3,2,512]{4,3,2,1,0:T(2,128)(2,1)} %stack.103), calls=%async_computation.4 | async-start | bytes 786432 | tf_op jit(solution)/shard_map/all_to_all | solution.py:140
  356.7 10.8 %all-to-all-done.4 = bf16[16,4,3,2,512]{4,3,2,1,0:T(2,128)(2,1)S(1)} async-done(((bf16[16,4,3,2,512]{4,3,2,1,0:T(2,128)(2,1)}), bf16[16,4,3,2,512]{4,3,2,1,0:T(2,128)(2,1)S(1)}, u32[]{:S(2)}, u32[]{:S(2)}) %all-to-all-start.4) | async-done | bytes 393248 | tf_op jit(solution)/shard_map/all_to_all | solution.py:140
  368.3 3.2 collective-permute-start
  371.5 2.8 collective-permute-start.1
  374.4 3.7 collective-permute-done.1
  398.3 7.9 %copy.123 = bf16[4,3,2,32,27,16]{3,2,1,0,5,4:T(2,128)(2,1)S(1)} copy(bf16[4,3,2,32,27,16]{5,3,2,1,0,4:T(8,128)(2,1)} %fusion.49) | data formatting | bytes 1327104 | tf_op jit(solution)/shard_map/stack | solution.py:80
  406.2 2.5 reshape_reshape.3
  408.7 1.7 convolution_add_fusion
  410.4 1.6 copy.124
  412.1 2.5 reshape.115
  414.5 2.7 reshape.116
  417.8 59.7 %psum.14 = f32[4,32]{1,0:T(4,128)S(1)} all-reduce(f32[4,32]{1,0:T(4,128)S(1)} %copy.125), channel_id=1, replica_groups=mesh['sec'=2,'seq'=32,'rep'=8] {'seq'}, use_global_device_ids=true, to_apply=%region_11.12 | all-reduce | flops 128 | bytes 1024 | tf_op jit(solution)/shard_map/psum | solution.py:156
  478.4 62.4 %psum.15 = f32[4,32]{1,0:T(4,128)S(1)} all-reduce(f32[4,32]{1,0:T(4,128)S(1)} %copy.127), channel_id=1, replica_groups=mesh['sec'=2,'seq'=32,'rep'=8] {'seq'}, use_global_device_ids=true, to_apply=%region_13.14 | all-reduce | flops 128 | bytes 1024 | tf_op jit(solution)/shard_map/psum | solution.py:158
  541.2 2.5 mul.94
  544.1 2.5 sub.70
  546.6 4.5 fusion.20
  (138 shorter events, 51.8 us)
Async XLA Ops:
  0.6 408.1 %copy-start = (bf16[3,3,3,16,512]{4,3,2,1,0:T(8,128)(2,1)S(1)}, bf16[3,3,3,16,512]{4,3,2,1,0:T(8,128)(2,1)}, u32[]{:S(2)}) copy-start(bf16[3,3,3,16,512]{4,3,2,1,0:T(8,128)(2,1)} %param.28) | copy-start | bytes 1327108
  0.6 77.9 %copy-start.2 = (bf16[4,24,48,128]{3,2,1,0:T(8,128)(2,1)S(1)}, bf16[4,24,48,128]{3,2,1,0:T(8,128)(2,1)}, u32[]{:S(2)}) copy-start(bf16[4,24,48,128]{3,2,1,0:T(8,128)(2,1)} %param.19) | copy-start | bytes 3538948
  142.7 61.9 %all-to-all-start.2 = ((bf16[32,3,48,128]{3,2,1,0:T(8,128)(2,1)}), bf16[32,3,48,128]{3,2,1,0:T(8,128)(2,1)S(1)}, u32[]{:S(2)}, u32[]{:S(2)}) async-start(bf16[32,3,48,128]{3,2,1,0:T(8,128)(2,1)} %bitcast.14), calls=%async_computation.2 | async-start | bytes 2359296 | tf_op jit(solution)/shard_map/all_to_all | solution.py:116
  146.9 1.6 copy-start.1
  229.9 14.1 %copy-start.11 = (s32[4]{0:T(128)S(1)}, s32[4]{0:T(128)}, u32[]{:S(2)}) copy-start(s32[4]{0:T(128)} %param.26) | copy-start | bytes 52
  229.9 14.1 %copy-start.3 = (f32[4,3072]{1,0:T(4,128)S(1)}, f32[4,3072]{1,0:T(4,128)}, u32[]{:S(2)}) copy-start(f32[4,3072]{1,0:T(4,128)} %param.22) | copy-start | bytes 147460
  229.9 14.1 %copy-start.4 = (f32[4,3072]{1,0:T(4,128)S(1)}, f32[4,3072]{1,0:T(4,128)}, u32[]{:S(2)}) copy-start(f32[4,3072]{1,0:T(4,128)} %param.21) | copy-start | bytes 147460
  238.0 82.3 %all-to-all-start.3 = ((bf16[1,3,1536,128]{3,1,0,2:T(4,128)(2,1)}), bf16[1,3,1536,128]{3,1,0,2:T(4,128)(2,1)S(1)}, u32[]{:S(2)}, u32[]{:S(2)}) async-start(bf16[1,3,1536,128]{3,1,0,2:T(4,128)(2,1)} %bitcast.225), calls=%async_computation.3 | async-start | bytes 3145728 | tf_op jit(solution)/shard_map/all_to_all | solution.py:118
  323.7 22.3 %copy-start.9 = (bf16[3072,64]{0,1:T(8,128)(2,1)S(1)}, bf16[3072,64]{0,1:T(8,128)(2,1)}, u32[]{:S(2)}) copy-start(bf16[3072,64]{0,1:T(8,128)(2,1)} %param.23) | copy-start | bytes 1179652
  323.7 22.3 %copy-start.12 = (f32[64]{0:T(128)S(1)}, f32[64]{0:T(128)}, u32[]{:S(2)}) copy-start(f32[64]{0:T(128)} %param.24) | copy-start | bytes 772
  324.0 24.7 %copy-start.5 = (f32[4,3,2,512]{3,2,1,0:T(2,128)S(1)}, f32[4,3,2,512]{3,2,1,0:T(2,128)}, u32[]{:S(2)}) copy-start(f32[4,3,2,512]{3,2,1,0:T(2,128)} %param.25) | copy-start | bytes 147460
  346.1 10.5 %copy-start.8 = (s32[64]{0:T(128)S(1)}, s32[64]{0:T(128)}, u32[]{:S(2)}) copy-start(s32[64]{0:T(128)} %param.27) | copy-start | bytes 772
  346.1 10.6 %copy-start.6 = (f32[512]{0:T(512)S(1)}, f32[512]{0:T(512)}, u32[]{:S(2)}) copy-start(f32[512]{0:T(512)} %param.31) | copy-start | bytes 6148
  346.1 28.2 %copy-start.7 = (f32[512]{0:T(512)S(1)}, f32[512]{0:T(512)}, u32[]{:S(2)}) copy-start(f32[512]{0:T(512)} %param.30) | copy-start | bytes 6148
  350.4 17.1 %all-to-all-start.4 = ((bf16[16,4,3,2,512]{4,3,2,1,0:T(2,128)(2,1)}), bf16[16,4,3,2,512]{4,3,2,1,0:T(2,128)(2,1)S(1)}, u32[]{:S(2)}, u32[]{:S(2)}) async-start(bf16[16,4,3,2,512]{4,3,2,1,0:T(2,128)(2,1)} %stack.103), calls=%async_computation.4 | async-start | bytes 786432 | tf_op jit(solution)/shard_map/all_to_all | solution.py:140
  368.3 6.2 %collective-permute-start = (bf16[4,3,1,512]{3,2,1,0:T(2,128)(2,1)S(1)}, bf16[4,3,1,512]{3,2,1,0:T(2,128)(2,1)S(1)}, u32[]{:S(2)}, u32[]{:S(2)}) collective-permute-start(bf16[4,3,1,512]{3,2,1,0:T(2,128)(2,1)S(1)} %get-tuple-element.89), channel_id=1, source_target_pairs={{0,8},{8,16},{16,24},{24,32},{32,40},{40,48},{48,56},{56,64},{64,7... | collective-permute-start | bytes 36872 | tf_op jit(solution)/shard_map/ppermute | solution.py:29
  371.5 6.6 %collective-permute-start.1 = (bf16[4,3,1,512]{3,2,1,0:T(2,128)(2,1)S(1)}, bf16[4,3,1,512]{3,2,1,0:T(2,128)(2,1)S(1)}, u32[]{:S(2)}, u32[]{:S(2)}) collective-permute-start(bf16[4,3,1,512]{3,2,1,0:T(2,128)(2,1)S(1)} %get-tuple-element.90), channel_id=1, source_target_pairs={{8,0},{16,8},{24,16},{32,24},{40,32},{48,40},{56,48},{64,56},{72,6... | collective-permute-start | bytes 36872 | tf_op jit(solution)/shard_map/ppermute | solution.py:31
  406.2 2.5 copy-start.10
